TPU v7x, 256 devices: a whole 4x4x8 slice. The times are simulated.
256 devices in a mesh: rows: 64 (over y, z, core), rhs: 4 (over x).
Axes of the slice: x: 4, y: 4, z: 8, core: 2. Of those that a mesh axis runs over, the one named last changes fastest.
Arguments:
- kernel_rows: bfloat16 [131072, 512], P(('rows', 'rhs')), may hold values from 0 to 1
- factor_blocks: bfloat16 [512, 8, 256, 256], P('rows'), may hold values from -0.125 to 0.125
- diag_inverse: bfloat16 [512, 256, 256], P('rows'), as said below
- pattern: int32 [512, 8], P('rows'), may hold values from 0 to 511, as said below
- live_counts: int32 [512], P('rows'), may hold values from 0 to 8, as said below
Outputs:
- solution: bfloat16 [131072, 512], P('rows', 'rhs')
Inputs may be any that keep to these rules, and one draw needn't show every extreme that they name: pattern[s, k] names a block row of a lower level than s; slot 0 of every block row above level 0 names a block row of the level just below; rows of level 0 hold 0. Block row t is held by index t // 8 of rows; the used slots of the block rows held by one index of rows name, for any one level, at most 1 distinct block rows held by any one other index. `live_counts`: 0 on level 0, from 1 to 8 on higher levels, 8 reached. `diag_inverse`: each block is the inverse of a well-conditioned diagonal block of the factor.
All inputs are finite; a program needn't handle non-finite values.
Results may differ from a plain program's by a relative error of at most 0.0058.
Values may be sent and summed in bfloat16 or wider, within the bound.
No kernel may reach another device: no remote copies, remote signals or barrier semaphores. Data moves between devices by JAX's collectives and lax.ppermute only.
A program may use at most 128 MiB of HBM per device.

v0:
```python
import jax
import jax.numpy as jnp
from jax import lax
from jax.sharding import PartitionSpec as P

LEV = 4


def shards(kernel_rows, factor_blocks, diag_inverse, pattern, live_counts):
    received = lax.all_to_all(kernel_rows, "rhs", split_axis=1, concat_axis=0, tiled=True)
    per_device = factor_blocks.shape[0]
    slot_count = factor_blocks.shape[1]
    block = factor_blocks.shape[2]
    width = received.shape[1]
    right_side = received.reshape(per_device, block, width)
    holders = lax.axis_size("rows")
    per_level = per_device // LEV
    level_size = holders * per_level
    level_of = pattern % per_device // per_level
    holder_of = pattern // per_device
    offset_of = pattern % per_level
    active = jnp.arange(slot_count)[None, :] < live_counts[:, None]
    position = holder_of * per_level + offset_of
    flat_index = level_of * level_size + position
    gathered_all = []
    solved_all = []
    for level_now in range(LEV):
        lower = level_now * per_level
        upper = lower + per_level
        if level_now == 0:
            summed_now = jnp.zeros((per_level, block, width), jnp.float32)
        else:
            available = jnp.concatenate(gathered_all, axis=0)
            picked = jnp.take(available, flat_index[lower:upper], axis=0, mode="clip")
            picked = jnp.where(active[lower:upper, :, None, None], picked, jnp.zeros_like(picked))
            summed_now = jnp.einsum(
                "bkij,bkjr->bir",
                factor_blocks[lower:upper],
                picked,
                preferred_element_type=jnp.float32,
            )
        residual = (right_side[lower:upper].astype(jnp.float32) - summed_now).astype(jnp.bfloat16)
        solved = jnp.einsum(
            "bij,bjr->bir", diag_inverse[lower:upper], residual, preferred_element_type=jnp.float32
        ).astype(jnp.bfloat16)
        solved_all.append(solved)
        if level_now + 1 < LEV:
            incoming = lax.all_gather(solved, "rows", axis=0, tiled=True)
            gathered_all.append(incoming)
    return jnp.concatenate(solved_all, axis=0).reshape(per_device * block, width)


def solution(mesh):
    placed = (
        P(("rows", "rhs"), None),
        P("rows", None, None, None),
        P("rows", None, None),
        P("rows", None),
        P("rows"),
    )
    return jax.shard_map(
        shards, mesh=mesh, in_specs=placed, out_specs=P("rows", "rhs"), check_vma=False
    )
```

profile of v0, /device:TPU:1, one launch (start us, length us, event | category | flops | bytes accessed | tf_op | source)
XLA Modules:
  0.0 339.4 jit_solution(18205425547887080133)
XLA Ops:
  6.5 1.3 copy.30
  7.8 13.2 %all_to_all.16 = bf16[512,4,128]{0,2,1:T(8,128)(2,1)S(1)} all-to-all(bf16[512,4,128]{0,2,1:T(8,128)(2,1)S(1)} %bitcast.60), channel_id=1, replica_groups=mesh['rows'=64,'rhs'=4] {'rhs'}, dimensions={1} | all-to-all | bytes 1048576 | tf_op jit(solution)/shard_map/all_to_all | solution.py:10
  21.0 0.1 fusion.84
  21.0 0.1 copy.31
  21.2 1.8 convolution_convert_fusion
  23.0 0.0 all-gather.6.cloned.1.call-start
  23.1 0.7 fusion.71
  23.8 0.1 reshape.28
  23.9 0.7 iota_compare_fusion
  24.6 0.1 copy.32
  24.7 0.1 copy.34
  24.9 84.1 %all-gather.4.cloned.1.call-done = bf16[128,256,128]{2,1,0:T(8,128)(2,1)} async-done(((bf16[2,256,128]{2,1,0:T(8,128)(2,1)}), bf16[128,256,128]{2,1,0:T(8,128)(2,1)}) %all-gather.4.cloned.1.call-update) | async-done | bytes 8388624 | tf_op jit(solution)/shard_map/all_gather | solution.py:48
  109.0 4.1 %gather_fusion = bf16[16,256,128]{2,1,0:T(8,128)(2,1)S(1)} fusion(bf16[128,256,128]{2,1,0:T(8,128)(2,1)} %all-gather.4.cloned.1.call-done, s32[1024]{0:T(1024)S(1)} %pad_clamp_fusion.2), kind=kCustom, calls=%fused_computation | custom fusion | bytes 2097216 | tf_op jit(solution)/shard_map/jit(_take)/gather | solution.py:34
  113.1 0.5 copy.33
  113.7 3.3 fusion.39
  117.0 0.1 reshape.36
  117.1 0.1 copy.36
  117.2 0.8 copy.38
  118.1 79.3 %all-gather.6.cloned.1.call-done = bf16[128,256,128]{2,1,0:T(8,128)(2,1)} async-done(((bf16[2,256,128]{2,1,0:T(8,128)(2,1)}), bf16[128,256,128]{2,1,0:T(8,128)(2,1)}) %all-gather.6.cloned.1.call-update) | async-done | bytes 8388624 | tf_op jit(solution)/shard_map/all_gather | solution.py:48
  197.4 13.9 %pad_maximum_fusion.1 = bf16[256,256,128]{2,1,0:T(8,128)(2,1)} fusion(bf16[128,256,128]{2,1,0:T(8,128)(2,1)} %all-gather.6.cloned.1.call-done, bf16[128,256,128]{2,1,0:T(8,128)(2,1)} %all-gather.4.cloned.1.call-done), kind=kLoop, calls=%fused_computation.4 | loop fusion | flops 8388608 | bytes 33554432 | tf_op jit(solution)/shard_map/concatenate | solution.py:33
  211.3 6.5 %gather_fusion.1 = bf16[16,256,128]{2,1,0:T(8,128)(2,1)S(1)} fusion(bf16[256,256,128]{2,1,0:T(8,128)(2,1)} %pad_maximum_fusion.1, s32[1024]{0:T(1024)S(1)} %pad_clamp_fusion.1), kind=kCustom, calls=%fused_computation.1 | custom fusion | bytes 2097216 | tf_op jit(solution)/shard_map/jit(_take)/gather | solution.py:34
  217.8 0.5 copy.37
  218.4 3.3 fusion.42
  221.7 0.1 reshape.44
  221.8 0.1 copy.40
  221.9 0.8 copy.42
  222.7 79.4 %all-gather.8.cloned.1.call-done = bf16[128,256,128]{2,1,0:T(8,128)(2,1)} async-done(((bf16[2,256,128]{2,1,0:T(8,128)(2,1)}), bf16[128,256,128]{2,1,0:T(8,128)(2,1)}) %all-gather.8.cloned.1.call-update) | async-done | bytes 8388624 | tf_op jit(solution)/shard_map/all_gather | solution.py:48
  302.1 17.7 %pad_maximum_fusion = bf16[384,256,128]{2,1,0:T(8,128)(2,1)} fusion(bf16[128,256,128]{2,1,0:T(8,128)(2,1)} %all-gather.8.cloned.1.call-done, bf16[128,256,128]{2,1,0:T(8,128)(2,1)} %all-gather.6.cloned.1.call-done, bf16[128,256,128]{2,1,0:T(8,128)(2,1)} %all-gather.4.cloned.1.call-done), kind=kLoop, calls=%fused_computation.3 | loop fusion | flops 25165824 | bytes 50331648 | tf_op jit(solution)/shard_map/concatenate | solution.py:33
  319.9 9.0 %gather_fusion.2 = bf16[16,256,128]{2,1,0:T(8,128)(2,1)S(1)} fusion(bf16[384,256,128]{2,1,0:T(8,128)(2,1)} %pad_maximum_fusion, s32[1024]{0:T(1024)S(1)} %pad_clamp_fusion), kind=kCustom, calls=%fused_computation.2 | custom fusion | bytes 2097216 | tf_op jit(solution)/shard_map/jit(_take)/gather | solution.py:34
  328.8 0.5 copy.41
  329.4 2.6 fusion.45
  332.0 0.9 pad_maximum_fusion.2
  (18 shorter events, 0.2 us)
Async XLA Ops:
  6.5 102.5 %all-gather.4.cloned.1.call-start = ((), (), s32[]{:S(2)}) async-start(), calls=%async_computation.1 | async-start | bytes 8519680 | tf_op jit(solution)/shard_map/all_gather | solution.py:48
  23.0 174.4 %all-gather.6.cloned.1.call-start = ((), (), s32[]{:S(2)}) async-start(), calls=%async_computation.2 | async-start | bytes 8519680 | tf_op jit(solution)/shard_map/all_gather | solution.py:48
  117.0 185.2 %all-gather.8.cloned.1.call-start = ((), (), s32[]{:S(2)}) async-start(), calls=%async_computation.3 | async-start | bytes 8519680 | tf_op jit(solution)/shard_map/all_gather | solution.py:48
  118.1 100.3 %copy-start.3 = (bf16[8,256,256]{2,1,0:T(8,128)(2,1)S(1)}, bf16[8,256,256]{2,1,0:T(8,128)(2,1)}, u32[]{:S(2)}) copy-start(bf16[8,256,256]{2,1,0:T(8,128)(2,1)} %param.7) | copy-start | bytes 3145732
  319.8 12.2 %copy-start = (bf16[2,256,128]{2,1,0:T(8,128)(2,1)S(1)}, bf16[2,256,128]{2,1,0:T(8,128)(2,1)}, u32[]{:S(2)}) copy-start(bf16[2,256,128]{2,1,0:T(8,128)(2,1)} %convolution_convert_fusion) | copy-start | bytes 393220
  319.9 12.2 %copy-start.1 = (bf16[2,256,128]{2,1,0:T(8,128)(2,1)S(1)}, bf16[2,256,128]{2,1,0:T(8,128)(2,1)}, u32[]{:S(2)}) copy-start(bf16[2,256,128]{2,1,0:T(8,128)(2,1)} %fusion.39) | copy-start | bytes 393220
  319.9 12.2 %copy-start.2 = (bf16[2,256,128]{2,1,0:T(8,128)(2,1)S(1)}, bf16[2,256,128]{2,1,0:T(8,128)(2,1)}, u32[]{:S(2)}) copy-start(bf16[2,256,128]{2,1,0:T(8,128)(2,1)} %fusion.42) | copy-start | bytes 393220
Sparse Core Ops, SparseCore 0:
  23.1 85.8 all-gather.3
  117.1 80.2 all-gather.5
  221.8 80.2 all-gather.7
where the time goes:
time: 340 us; the launch traced here: 339 us
  waiting for transfers between devices  243 us (71%)
  other arithmetic  34 us (10%)
  local copies, waits for them, and re-layouts  25 us (7%)
  between operations  13.3 us (4%)
  blocking collectives  13.2 us (4%)
  matrix products  11 us (3%)
    all_gather x3, waiting for transfers between devices, shards(): incoming = lax.all_gather(solved, 'rows', axis=0, tiled=True)  243 us
    concatenate x2, other arithmetic, shards(): available = jnp.concatenate(gathered_all, axis=0)  31.6 us
    gather x6, local copies, waits for them, and re-layouts, shards(): picked = jnp.take(available, flat_index[lower:upper], axis=0, mode='clip')  21.2 us
    all_to_all x1, blocking collectives, shards(): lax.all_to_all(kernel_rows, 'rhs', split_axis=1, concat_axis=0, tiled=True)  13.2 us
    dot_general x4, matrix products, shards(): jnp.einsum('bij,bjr->bir', diag_inverse[lower:upper], residual, preferred...  11 us
  transfers between devices with their start and end apart: 3, of which 3 were waited for; matrix products, arithmetic and copies ran while one was open for 1% of the time, Pallas kernels for 0%

commit v1 on v0

--- a/solution.py
+++ b/solution.py
@@ -4,6 +4,11 @@
 from jax.sharding import PartitionSpec as P
 
 LEV = 4
+
+
+def gather_from_all(x, axis, dim):
+    copies = jnp.concatenate([x] * lax.axis_size(axis), axis=dim)
+    return lax.all_to_all(copies, axis, dim, dim, tiled=True)
 
 
 def shards(kernel_rows, factor_blocks, diag_inverse, pattern, live_counts):
@@ -45,7 +50,7 @@
         ).astype(jnp.bfloat16)
         solved_all.append(solved)
         if level_now + 1 < LEV:
-            incoming = lax.all_gather(solved, "rows", axis=0, tiled=True)
+            incoming = gather_from_all(solved, "rows", 0)
             gathered_all.append(incoming)
     return jnp.concatenate(solved_all, axis=0).reshape(per_device * block, width)
 

time: 340 us -> 788 us (2.32)
  waiting for transfers between devices: 243 us -> 556 us
  local copies, waits for them, and re-layouts: 25 us -> 148 us
  starting transfers between devices: 0.09 us -> 26 us
  between operations: 13.3 us -> 0.28 us
    all_to_all x0 -> x3, waiting for transfers between devices: none -> 556 us  [gather_from_all(): return lax.all_to_all(copies, axis, dim, dim, tiled=True)]
    all_gather x3 -> x0, waiting for transfers between devices: 243 us -> none  [shards(): incoming = lax.all_gather(solved, 'rows', axis=0, tiled=True)]
    unnamed x9 -> x191, local copies, waits for them, and re-layouts: 1.27 us -> 124 us
    all_to_all x0 -> x3, starting transfers between devices: none -> 26 us  [gather_from_all(): return lax.all_to_all(copies, axis, dim, dim, tiled=True)]
  transfers between devices with their start and end apart: 3 -> 3, of which waited for: 3 -> 3; matrix products, arithmetic and copies ran while one was open for 1% -> 0% of each run, Pallas kernels for 0% -> 0%
where the time goes in v1:
time: 788 us; the launch traced here: 787 us
  waiting for transfers between devices  556 us (71%)
  local copies, waits for them, and re-layouts  148 us (19%)
  other arithmetic  32.6 us (4%)
  starting transfers between devices  26 us (3%)
  blocking collectives  13.2 us (2%)
  matrix products  11 us (1%)
    all_to_all x3, waiting for transfers between devices, gather_from_all(): return lax.all_to_all(copies, axis, dim, dim, tiled=True)  556 us
    unnamed x191, local copies, waits for them, and re-layouts  124 us
    concatenate x2, other arithmetic, shards(): available = jnp.concatenate(gathered_all, axis=0)  31.6 us
    all_to_all x3, starting transfers between devices, gather_from_all(): return lax.all_to_all(copies, axis, dim, dim, tiled=True)  26 us
    gather x6, local copies, waits for them, and re-layouts, shards(): picked = jnp.take(available, flat_index[lower:upper], axis=0, mode='clip')  21.1 us
  transfers between devices with their start and end apart: 3, of which 3 were waited for; matrix products, arithmetic and copies ran while one was open for 0% of the time, Pallas kernels for 0%

profile of v1, /device:TPU:1, one launch (start us, length us, event | category | flops | bytes accessed | tf_op | source)
XLA Modules:
  0.0 786.9 jit_solution(2433841736740285781)
XLA Ops:
  0.0 1.3 copy.16
  1.3 13.2 %all_to_all.31 = bf16[512,4,128]{0,2,1:T(8,128)(2,1)S(1)} all-to-all(bf16[512,4,128]{0,2,1:T(8,128)(2,1)S(1)} %bitcast.64), channel_id=1, replica_groups=mesh['rows'=64,'rhs'=4] {'rhs'}, dimensions={1} | all-to-all | bytes 1048576 | tf_op jit(solution)/shard_map/all_to_all | solution.py:15
  14.6 1.8 constant_dynamic-update-slice_fusion.63
  34.8 0.7 constant_dynamic-update-slice_fusion.34
  40.7 0.7 constant_dynamic-update-slice_fusion.25
  49.3 0.7 constant_dynamic-update-slice_fusion.12
  55.9 0.7 constant_dynamic-update-slice_fusion.2
  56.6 0.7 constant_dynamic-update-slice_fusion.1
  57.9 13.9 %all-to-all-start.1 = ((bf16[128,256,128]{2,1,0:T(8,128)(2,1)}), bf16[128,256,128]{2,1,0:T(8,128)(2,1)}, u32[]{:S(2)}, u32[]{:S(2)}) async-start(bf16[128,256,128]{2,1,0:T(8,128)(2,1)} %constant_dynamic-update-slice_fusion), calls=%async_computation.1 | async-start | bytes 16777216 | tf_op jit(solution)/shard_map/all_to_all | solution.py:11
  72.3 185.3 %all-to-all-done.1 = bf16[128,256,128]{2,1,0:T(8,128)(2,1)} async-done(((bf16[128,256,128]{2,1,0:T(8,128)(2,1)}), bf16[128,256,128]{2,1,0:T(8,128)(2,1)}, u32[]{:S(2)}, u32[]{:S(2)}) %all-to-all-start.1) | async-done | bytes 8388640 | tf_op jit(solution)/shard_map/all_to_all | solution.py:11
  257.6 4.1 gather_fusion
  262.2 3.3 constant_dynamic-update-slice_fusion.127
  283.9 0.7 constant_dynamic-update-slice_fusion.98
  289.8 0.7 constant_dynamic-update-slice_fusion.89
  298.4 0.7 constant_dynamic-update-slice_fusion.76
  304.9 0.7 constant_dynamic-update-slice_fusion.66
  305.6 0.7 constant_dynamic-update-slice_fusion.65
  306.9 6.1 all-to-all-start.2
  313.4 185.4 %all-to-all-done.2 = bf16[128,256,128]{2,1,0:T(8,128)(2,1)} async-done(((bf16[128,256,128]{2,1,0:T(8,128)(2,1)}), bf16[128,256,128]{2,1,0:T(8,128)(2,1)}, u32[]{:S(2)}, u32[]{:S(2)}) %all-to-all-start.2) | async-done | bytes 8388640 | tf_op jit(solution)/shard_map/all_to_all | solution.py:11
  498.8 13.9 %pad_maximum_fusion.1 = bf16[256,256,128]{2,1,0:T(8,128)(2,1)} fusion(bf16[128,256,128]{2,1,0:T(8,128)(2,1)} %all-to-all-done.2, bf16[128,256,128]{2,1,0:T(8,128)(2,1)} %all-to-all-done.1), kind=kLoop, calls=%fused_computation.4 | loop fusion | flops 8388608 | bytes 33554432 | tf_op jit(solution)/shard_map/concatenate | solution.py:38
  512.7 6.5 gather_fusion.1
  519.8 3.3 constant_dynamic-update-slice_fusion.191
  547.3 0.7 constant_dynamic-update-slice_fusion.153
  555.9 0.7 constant_dynamic-update-slice_fusion.140
  562.5 0.7 constant_dynamic-update-slice_fusion.130
  563.1 0.7 constant_dynamic-update-slice_fusion.129
  564.5 6.1 all-to-all-start.3
  570.9 185.4 %all-to-all-done.3 = bf16[128,256,128]{2,1,0:T(8,128)(2,1)} async-done(((bf16[128,256,128]{2,1,0:T(8,128)(2,1)}), bf16[128,256,128]{2,1,0:T(8,128)(2,1)}, u32[]{:S(2)}, u32[]{:S(2)}) %all-to-all-start.3) | async-done | bytes 8388640 | tf_op jit(solution)/shard_map/all_to_all | solution.py:11
  756.3 17.7 %pad_maximum_fusion = bf16[384,256,128]{2,1,0:T(8,128)(2,1)} fusion(bf16[128,256,128]{2,1,0:T(8,128)(2,1)} %all-to-all-done.3, bf16[128,256,128]{2,1,0:T(8,128)(2,1)} %all-to-all-done.2, bf16[128,256,128]{2,1,0:T(8,128)(2,1)} %all-to-all-done.1), kind=kLoop, calls=%fused_computation.3 | loop fusion | flops 25165824 | bytes 50331648 | tf_op jit(solution)/shard_map/concatenate | solution.py:38
  774.0 8.9 %gather_fusion.2 = bf16[16,256,128]{2,1,0:T(8,128)(2,1)S(1)} fusion(bf16[384,256,128]{2,1,0:T(8,128)(2,1)} %pad_maximum_fusion, s32[1024]{0:T(1024)S(1)} %pad_clamp_fusion), kind=kCustom, calls=%fused_computation.2 | custom fusion | bytes 2097216 | tf_op jit(solution)/shard_map/jit(_take)/gather | solution.py:39
  783.5 2.6 fusion.45
  786.1 0.9 pad_maximum_fusion.2
  (200 shorter events, 117.7 us)
Async XLA Ops:
  57.9 13.9 %copy-start = (s32[8,8]{1,0:T(8,128)S(1)}, s32[8,8]{1,0:T(8,128)}, u32[]{:S(2)}) copy-start(s32[8,8]{1,0:T(8,128)} %param.8) | copy-start | bytes 772
  57.9 14.0 %copy-start.1 = (s32[8]{0:T(128)S(1)}, s32[8]{0:T(128)}, u32[]{:S(2)}) copy-start(s32[8]{0:T(128)} %param.9) | copy-start | bytes 100
  57.9 199.7 %all-to-all-start.1 = ((bf16[128,256,128]{2,1,0:T(8,128)(2,1)}), bf16[128,256,128]{2,1,0:T(8,128)(2,1)}, u32[]{:S(2)}, u32[]{:S(2)}) async-start(bf16[128,256,128]{2,1,0:T(8,128)(2,1)} %constant_dynamic-update-slice_fusion), calls=%async_computation.1 | async-start | bytes 16777216 | tf_op jit(solution)/shard_map/all_to_all | solution.py:11
  306.9 191.9 %all-to-all-start.2 = ((bf16[128,256,128]{2,1,0:T(8,128)(2,1)}), bf16[128,256,128]{2,1,0:T(8,128)(2,1)}, u32[]{:S(2)}, u32[]{:S(2)}) async-start(bf16[128,256,128]{2,1,0:T(8,128)(2,1)} %constant_dynamic-update-slice_fusion.64), calls=%async_computation.2 | async-start | bytes 16777216 | tf_op jit(solution)/shard_map/all_to_all | solution.py:11
  564.5 191.9 %all-to-all-start.3 = ((bf16[128,256,128]{2,1,0:T(8,128)(2,1)}), bf16[128,256,128]{2,1,0:T(8,128)(2,1)}, u32[]{:S(2)}, u32[]{:S(2)}) async-start(bf16[128,256,128]{2,1,0:T(8,128)(2,1)} %constant_dynamic-update-slice_fusion.128), calls=%async_computation.3 | async-start | bytes 16777216 | tf_op jit(solution)/shard_map/all_to_all | solution.py:11
